TPU v7x, 256 devices: a whole 4x4x8 slice. The times are simulated.
256 devices in a mesh: seq: 64 (over z, y, core), tensor: 4 (over x).
Axes of the slice: x: 4, y: 4, z: 8, core: 2. Of those that a mesh axis runs over, the one named last changes fastest.
Arguments:
- new_states: bfloat16 [4, 128, 1024], P(None, None, 'tensor'), may hold values from -6 to 6
- self_query: bfloat16 [1024, 1024], P(None, 'tensor'), may hold values from -0.1875 to 0.1875
- self_key: bfloat16 [1024, 1024], P(None, 'tensor'), may hold values from -0.375 to 0.375
- self_value: bfloat16 [1024, 1024], P(None, 'tensor'), may hold values from -0.1875 to 0.1875
- self_output: bfloat16 [1024, 1024], P('tensor'), may hold values from -0.1875 to 0.1875
- cross_query: bfloat16 [1024, 1024], P(None, 'tensor'), may hold values from -0.1875 to 0.1875
- cross_output: bfloat16 [1024, 1024], P('tensor'), may hold values from -0.1875 to 0.1875
- feed_up: bfloat16 [1024, 4096], P(None, 'tensor'), may hold values from -0.1875 to 0.1875
- feed_down: bfloat16 [4096, 1024], P('tensor'), may hold values from -0.09375 to 0.09375
- norm_self: float32 [1024], replicated, may hold values from 0.25 to 1.75
- norm_cross: float32 [1024], replicated, may hold values from 0.25 to 1.75
- norm_feed: float32 [1024], replicated, may hold values from 0.25 to 1.75
- self_cache: bfloat16 [1536, 2, 128, 1024], P('seq', None, None, 'tensor'), may hold values from -240 to 240
- cross_cache: bfloat16 [128, 2, 512, 1024], P(None, None, 'seq', 'tensor'), may hold values from -240 to 240
- cache_lengths: int32 [128], replicated, may hold values from 1 to 16384, as said below
- page_table: int32 [128, 128], replicated, may hold values from -1 to 1535, as said below
- request_order: int32 [128], replicated, may hold values from 0 to 127, each once
- encoder_lengths: int32 [128], replicated, may hold values from 1 to 512, as said below
Outputs:
- out: bfloat16 [4, 128, 1024], P(None, None, 'tensor')
Inputs may be any that keep to these rules, and one draw needn't show every extreme that they name: `cache_lengths`: one request has exactly 16384 cached tokens. `page_table`: row r holds the slots of request r's pages in order: its first ceil(cache_lengths[r] / 128) entries are slots, page p holding positions p * 128 to (p + 1) * 128 - 1, and no slot appears twice in the table; the other entries are -1. Slot s belongs to seq index s // 24. `encoder_lengths`: one request has exactly 512 encoder positions.
All inputs are finite; a program needn't handle non-finite values.
Results may differ from a plain program's by a relative error of at most 0.014.
The roundings to bfloat16 on the way count: a program that leaves them out, or rounds other values in their place, can miss the bound.
Values may be sent and summed in bfloat16 or wider, within the bound.
No kernel may reach another device: no remote copies, remote signals or barrier semaphores. Data moves between devices by JAX's collectives and lax.ppermute only.
A program may use at most 64 MiB of HBM per device.

v0:
```python
import jax
import jax.numpy as jnp
from jax import lax
from jax.sharding import PartitionSpec as P

HEAD_DIM = 64
EPSILON = 1e-05
NEG_FILL = -1e30


def layer_norm(summed, gain):
    center = jnp.mean(summed, axis=-1, keepdims=True)
    spread = jnp.mean(summed * summed, axis=-1, keepdims=True) - center * center
    return (summed - center) * lax.rsqrt(spread + EPSILON) * gain


def global_max(local_max, size):
    result = local_max
    distance = 1
    while distance < size:
        pairs = [(i, i ^ distance) for i in range(size)]
        result = jnp.maximum(result, lax.ppermute(result, "seq", pairs))
        distance *= 2
    return result


def global_totals(denom, numer):
    packed = jnp.concatenate([numer.reshape(-1), denom.reshape(-1)])
    packed = lax.psum(packed, "seq")
    count = numer.size
    return (packed[count:].reshape(denom.shape), packed[:count].reshape(numer.shape))


def reduce_norm(residual, partial_value, gain):
    width = residual.shape[1]
    total = lax.psum(partial_value, "tensor")
    full = layer_norm(residual.astype(jnp.float32) + total, gain).astype(jnp.bfloat16)
    columns = width // lax.axis_size("tensor")
    return (full, lax.dynamic_slice_in_dim(full, lax.axis_index("tensor") * columns, columns, 1))


def on_device(
    new_states,
    self_query,
    self_key,
    self_value,
    self_output,
    cross_query,
    cross_output,
    feed_up,
    feed_down,
    norm_self,
    norm_cross,
    norm_feed,
    self_cache,
    cross_cache,
    cache_lengths,
    page_table,
    request_order,
    encoder_lengths,
):
    states = lax.all_gather(new_states, "tensor", axis=2, tiled=True)
    steps, requests, width = states.shape
    flat = states.reshape(steps * requests, width)
    local_width = self_query.shape[1]
    local_heads = local_width // HEAD_DIM
    scaling = HEAD_DIM ** (-0.5)
    queries = (jnp.dot(flat, self_query, preferred_element_type=jnp.float32) * scaling).astype(
        jnp.bfloat16
    )
    new_keys = jnp.dot(flat, self_key, preferred_element_type=jnp.float32).astype(jnp.bfloat16)
    new_values = jnp.dot(flat, self_value, preferred_element_type=jnp.float32).astype(jnp.bfloat16)
    query_grid = queries.reshape(steps, requests, local_heads, HEAD_DIM)
    key_grid = new_keys.reshape(steps, requests, local_heads, HEAD_DIM)
    value_grid = new_values.reshape(steps, requests, local_heads, HEAD_DIM)
    slot_count = self_cache.shape[0]
    page_width = self_cache.shape[2]
    max_pages = page_table.shape[1]
    seq_index = lax.axis_index("seq")
    seq_size = lax.axis_size("seq")
    flat_table = page_table.reshape(-1)
    entry_ids = jnp.arange(requests * max_pages, dtype=jnp.int32)
    entry_request = entry_ids // max_pages
    entry_page = entry_ids % max_pages
    slot_ids = seq_index * slot_count + jnp.arange(slot_count, dtype=jnp.int32)
    matches = flat_table[None, :] == slot_ids[:, None]
    slot_live = jnp.any(matches, axis=1)
    slot_owner = jnp.sum(jnp.where(matches, entry_request[None, :], 0), axis=1)
    slot_page = jnp.sum(jnp.where(matches, entry_page[None, :], 0), axis=1)
    request_ids = jnp.arange(requests, dtype=jnp.int32)
    slot_length = jnp.sum(
        jnp.where(slot_owner[:, None] == request_ids[None, :], cache_lengths[None, :], 0), axis=1
    )
    positions = slot_page[:, None] * page_width + jnp.arange(page_width, dtype=jnp.int32)[None, :]
    slot_valid = slot_live[:, None] & (positions < slot_length[:, None])
    slot_rows = slot_live[:, None] & (request_order[None, :] == slot_owner[:, None])
    rows_half = slot_rows.astype(jnp.bfloat16)
    rows_wide = slot_rows.astype(jnp.float32)
    slot_query = jnp.einsum(
        "pb,sbc->psc",
        rows_half,
        queries.reshape(steps, requests, local_width),
        preferred_element_type=jnp.float32,
    ).astype(jnp.bfloat16)
    slot_query = slot_query.reshape(slot_count, steps, local_heads, HEAD_DIM)
    cache_keys = self_cache[:, 0].reshape(slot_count, page_width, local_heads, HEAD_DIM)
    cache_values = self_cache[:, 1].reshape(slot_count, page_width, local_heads, HEAD_DIM)
    cache_scores = jnp.einsum(
        "pshd,pkhd->pshk", slot_query, cache_keys, preferred_element_type=jnp.float32
    )
    valid_grid = slot_valid[:, None, None, :]
    slot_max = jnp.max(jnp.where(valid_grid, cache_scores, NEG_FILL), axis=3)
    row_max = jnp.max(
        jnp.where(slot_rows[:, None, :, None], slot_max[:, :, None, :], NEG_FILL), axis=0
    )
    causal = jnp.arange(steps)[None, :] <= jnp.arange(steps)[:, None]
    new_scores = jnp.einsum(
        "tbhd,ubhd->bhtu", query_grid, key_grid, preferred_element_type=jnp.float32
    )
    new_scores = jnp.where(causal, new_scores, NEG_FILL)
    new_max = jnp.transpose(jnp.max(new_scores, axis=3), (2, 0, 1))
    top = global_max(jnp.maximum(row_max, new_max), seq_size)
    slot_top = jnp.einsum("pb,sbh->psh", rows_wide, top, precision=lax.Precision.HIGHEST)
    cache_weights = jnp.exp(jnp.where(valid_grid, cache_scores - slot_top[..., None], NEG_FILL))
    cache_denom = jnp.sum(cache_weights, axis=3)
    cache_numer = jnp.einsum(
        "pshk,pkhd->pshd",
        cache_weights.astype(jnp.bfloat16),
        cache_values,
        preferred_element_type=jnp.float32,
    )
    row_denom = jnp.einsum("pb,psh->sbh", rows_wide, cache_denom, precision=lax.Precision.HIGHEST)
    row_numer = jnp.einsum("pb,pshd->sbhd", rows_wide, cache_numer, precision=lax.Precision.HIGHEST)
    total_denom, total_numer = global_totals(row_denom, row_numer)
    top_new = jnp.transpose(top, (1, 2, 0))[..., None]
    new_weights = jnp.where(causal, jnp.exp(new_scores - top_new), 0.0)
    new_denom = jnp.transpose(jnp.sum(new_weights, axis=3), (2, 0, 1))
    new_numer = jnp.einsum(
        "bhtu,ubhd->tbhd",
        new_weights.astype(jnp.bfloat16),
        value_grid,
        preferred_element_type=jnp.float32,
    )
    self_attn = ((total_numer + new_numer) / (total_denom + new_denom)[..., None]).astype(
        jnp.bfloat16
    )
    partial_value = jnp.dot(
        self_attn.reshape(steps * requests, local_width),
        self_output,
        preferred_element_type=jnp.float32,
    )
    first_full, first_share = reduce_norm(flat, partial_value, norm_self)
    cross_queries = (
        jnp.dot(first_full, cross_query, preferred_element_type=jnp.float32) * scaling
    ).astype(jnp.bfloat16)
    cross_grid = cross_queries.reshape(steps, requests, local_heads, HEAD_DIM)
    order_rows = (request_order[:, None] == request_ids[None, :]).astype(jnp.bfloat16)
    request_query = jnp.einsum(
        "br,sbhd->srhd", order_rows, cross_grid, preferred_element_type=jnp.float32
    ).astype(jnp.bfloat16)
    enc_local = cross_cache.shape[2]
    enc_keys = cross_cache[:, 0].reshape(requests, enc_local, local_heads, HEAD_DIM)
    enc_values = cross_cache[:, 1].reshape(requests, enc_local, local_heads, HEAD_DIM)
    enc_positions = seq_index * enc_local + jnp.arange(enc_local, dtype=jnp.int32)
    enc_valid = (enc_positions[None, :] < encoder_lengths[:, None])[None, :, None, :]
    enc_scores = jnp.einsum(
        "srhd,rehd->srhe", request_query, enc_keys, preferred_element_type=jnp.float32
    )
    enc_top = global_max(jnp.max(jnp.where(enc_valid, enc_scores, NEG_FILL), axis=3), seq_size)
    enc_weights = jnp.exp(jnp.where(enc_valid, enc_scores - enc_top[..., None], NEG_FILL))
    enc_numer_local = jnp.einsum(
        "srhe,rehd->srhd",
        enc_weights.astype(jnp.bfloat16),
        enc_values,
        preferred_element_type=jnp.float32,
    )
    enc_denom, enc_numer = global_totals(jnp.sum(enc_weights, axis=3), enc_numer_local)
    enc_attn = (enc_numer / enc_denom[..., None]).astype(jnp.bfloat16)
    cross_attn = jnp.einsum(
        "br,srhd->sbhd", order_rows, enc_attn, preferred_element_type=jnp.float32
    ).astype(jnp.bfloat16)
    partial_value = jnp.dot(
        cross_attn.reshape(steps * requests, local_width),
        cross_output,
        preferred_element_type=jnp.float32,
    )
    second_full, second_share = reduce_norm(first_full, partial_value, norm_cross)
    ffn_hidden = jax.nn.gelu(
        jnp.dot(second_full, feed_up, preferred_element_type=jnp.float32), approximate=False
    ).astype(jnp.bfloat16)
    ignored, out_share = reduce_norm(
        second_full, jnp.dot(ffn_hidden, feed_down, preferred_element_type=jnp.float32), norm_feed
    )
    return out_share.reshape(steps, requests, out_share.shape[1])


def solution(mesh):
    in_specs = (
        P(None, None, "tensor"),
        P(None, "tensor"),
        P(None, "tensor"),
        P(None, "tensor"),
        P("tensor", None),
        P(None, "tensor"),
        P("tensor", None),
        P(None, "tensor"),
        P("tensor", None),
        P(),
        P(),
        P(),
        P("seq", None, None, "tensor"),
        P(None, None, "seq", "tensor"),
        P(),
        P(),
        P(),
        P(),
    )
    out_specs = P(None, None, "tensor")
    return jax.shard_map(
        on_device, mesh=mesh, in_specs=in_specs, out_specs=out_specs, check_vma=False
    )
```

profile of v0, /device:TPU:1, one launch (start us, length us, event | category | flops | bytes accessed | tf_op | source)
XLA Modules:
  0.0 771.3 jit_solution(12482341161338022725)
XLA Ops:
  7.3 3.9 fusion.133
  11.2 2.6 copy.115
  15.2 24.1 %all-gather.2.cloned.1.call-done = bf16[4,128,1024]{2,1,0:T(8,128)(2,1)} async-done(((bf16[4,128,256]{2,1,0:T(8,128)(2,1)}), bf16[4,128,1024]{2,1,0:T(8,128)(2,1)}) %all-gather.2.cloned.1.call-update) | async-done | bytes 1048592 | tf_op jit(solution)/shard_map/all_gather | solution.py:62
  42.3 2.0 select_reduce_fusion.2
  44.5 2.2 convolution_convert_fusion.3
  46.6 2.0 reshape.291
  48.7 3.0 fusion.61
  53.5 2.4 collective-permute-start
  59.2 2.7 collective-permute-start.2
  65.7 2.3 collective-permute-start.4
  68.0 2.6 copy.164
  70.6 4.0 collective-permute-start.5
  74.6 2.2 convolution_convert_fusion.2
  76.8 2.0 reshape.292
  80.2 2.4 convolution_bitcast_fusion.3
  86.7 1.9 pad_maximum_fusion
  90.5 1.9 fusion.59
  93.8 179.4 %all-reduce.6.cloned.1.call-done = f32[133120]{0:T(1024)} async-done(((f32[133120]{0:T(1024)}), f32[133120]{0:T(1024)}) %all-reduce.6.cloned.1.call-update) | async-done | bytes 532496 | tf_op jit(solution)/shard_map/psum | solution.py:29
  273.2 1.9 slice.54
  278.7 2.5 copy.138
  286.9 2.3 fusion.134
  289.2 2.2 copy.165
  291.5 3.4 copy.145
  294.9 55.6 %all-reduce.8.cloned.1.call-done = f32[512,1024]{1,0:T(8,128)} async-done(((f32[512,1024]{1,0:T(8,128)}), f32[512,1024]{1,0:T(8,128)}) %all-reduce.8.cloned.1.call-update) | async-done | bytes 2097168 | tf_op jit(solution)/shard_map/psum | solution.py:36
  350.6 2.2 fusion.48
  358.2 3.2 select_reduce_fusion
  364.9 6.3 collective-permute-done.7
  371.2 2.8 collective-permute-start.8
  374.1 5.4 collective-permute-done.8
  380.9 4.5 collective-permute-done.9
  385.5 2.4 collective-permute-start.10
  387.8 11.5 %collective-permute-done.10 = f32[4,128,4]{0,2,1:T(4,128)S(1)} collective-permute-done((f32[4,128,4]{0,2,1:T(4,128)S(1)}, f32[4,128,4]{0,2,1:T(4,128)S(1)}, u32[]{:S(2)}, u32[]{:S(2)}) %collective-permute-start.10) | collective-permute-done | bytes 8224 | tf_op jit(solution)/shard_map/ppermute | solution.py:22
  399.4 6.2 collective-permute-start.11
  405.6 2.2 copy.166
  407.8 3.4 copy.147
  411.2 2.9 collective-permute-done.11
  415.9 2.4 fusion.50
  421.1 2.5 convolution_bitcast_fusion
  424.8 2.5 reshape.280
  427.4 1.9 pad_maximum_fusion.1
  429.3 182.5 %all-reduce.10.cloned.1.call-done = f32[133120]{0:T(1024)} async-done(((f32[133120]{0:T(1024)}), f32[133120]{0:T(1024)}) %all-reduce.10.cloned.1.call-update) | async-done | bytes 532496 | tf_op jit(solution)/shard_map/psum | solution.py:29
  611.8 1.9 slice.56
  613.7 2.5 reshape.282
  620.9 63.5 %all-reduce.12.cloned.1.call-done = f32[512,1024]{1,0:T(8,128)} async-done(((f32[512,1024]{1,0:T(8,128)}), f32[512,1024]{1,0:T(8,128)}) %all-reduce.12.cloned.1.call-update) | async-done | bytes 2097168 | tf_op jit(solution)/shard_map/psum | solution.py:36
  684.4 2.2 fusion.49
  688.0 9.5 %fusion.16 = f32[512,1024]{1,0:T(8,128)} fusion(bf16[1024,1024]{1,0:T(8,128)(2,1)S(1)} %copy-done, bf16[512,1024]{1,0:T(8,128)(2,1)} %multiply_convert_fusion, bf16[1024,1024]{1,0:T(8,128)(2,1)} %param.25), kind=kOutput, calls=%fused_computation.49 | convolution fusion | flops 2181562368 | bytes 7340032 | tf_op jit(solution)/shard_map/dot_general | solution.py:192
  698.4 62.9 %all-reduce.14.cloned.1.call-done = f32[512,1024]{1,0:T(8,128)} async-done(((f32[512,1024]{1,0:T(8,128)}), f32[512,1024]{1,0:T(8,128)}) %all-reduce.14.cloned.1.call-update) | async-done | bytes 2097168 | tf_op jit(solution)/shard_map/psum | solution.py:36
  761.3 2.0 fusion.132
  (141 shorter events, 56.6 us)
Async XLA Ops:
  6.5 681.5 %copy-start = (bf16[1024,1024]{1,0:T(8,128)(2,1)S(1)}, bf16[1024,1024]{1,0:T(8,128)(2,1)}, u32[]{:S(2)}) copy-start(bf16[1024,1024]{1,0:T(8,128)(2,1)} %param.26) | copy-start | bytes 6291460
  6.5 32.7 %all-gather.2.cloned.1.call-start = ((), (), s32[]{:S(2)}) async-start(), calls=%async_computation | async-start | bytes 1310720 | tf_op jit(solution)/shard_map/all_gather | solution.py:62
  7.3 265.9 %all-reduce.6.cloned.1.call-start = ((), (), s32[]{:S(2)}) async-start(), calls=%async_computation.1 | async-start | bytes 1064960 | tf_op jit(solution)/shard_map/psum | solution.py:29
  11.2 2.7 copy-start.12
  11.2 3.3 copy-start.19
  11.2 3.9 copy-start.13
  11.2 28.1 %copy-start.17 = (bf16[1024,256]{1,0:T(8,128)(2,1)S(1)}, bf16[1024,256]{1,0:T(8,128)(2,1)}, u32[]{:S(2)}) copy-start(bf16[1024,256]{1,0:T(8,128)(2,1)} %param.19) | copy-start | bytes 1572868
  40.9 3.5 copy-start.3
  53.5 3.2 collective-permute-start
  56.7 2.5 collective-permute-start.1
  59.2 4.0 collective-permute-start.2
  63.2 2.5 collective-permute-start.3
  65.7 4.9 collective-permute-start.4
  70.6 8.2 %collective-permute-start.5 = (f32[4,128,4]{1,2,0:T(4,128)S(1)}, f32[4,128,4]{1,2,0:T(4,128)S(1)}, u32[]{:S(2)}, u32[]{:S(2)}) collective-permute-start(f32[4,128,4]{1,2,0:T(4,128)S(1)} %max.44), channel_id=1, source_target_pairs={{0,128},{4,132},{8,136},{12,140},{16,144},{20,148},{24,152},{28,15... | collective-permute-start | bytes 24584 | tf_op jit(solution)/shard_map/ppermute | solution.py:22
  88.6 261.9 %all-reduce.8.cloned.1.call-start = ((), (), s32[]{:S(2)}) async-start(), calls=%async_computation.2 | async-start | bytes 4194304 | tf_op jit(solution)/shard_map/psum | solution.py:36
  273.2 4.5 slice-start
  277.7 6.2 copy-start.7
  277.7 6.2 copy-start.8
  283.9 1.1 copy-start.10
  286.8 325.0 %all-reduce.10.cloned.1.call-start = ((), (), s32[]{:S(2)}) async-start(), calls=%async_computation.3 | async-start | bytes 1064960 | tf_op jit(solution)/shard_map/psum | solution.py:29
  286.8 8.0 %copy-start.16 = (s32[128]{0:T(128)S(1)}, s32[128]{0:T(128)}, u32[]{:S(2)}) copy-start(s32[128]{0:T(128)} %param.35) | copy-start | bytes 1540
  286.9 63.7 %copy-start.4 = (bf16[4,128,1024]{2,1,0:T(8,128)(2,1)S(1)}, bf16[4,128,1024]{2,1,0:T(8,128)(2,1)}, u32[]{:S(2)}) copy-start(bf16[4,128,1024]{2,1,0:T(8,128)(2,1)} %all-gather.2.cloned.1.call-done) | copy-start | bytes 3145732
  291.5 61.3 %copy-start.14 = (f32[1024]{0:T(1024)S(1)}, f32[1024]{0:T(1024)}, u32[]{:S(2)}) copy-start(f32[1024]{0:T(1024)} %param.27) | copy-start | bytes 12292
  350.5 2.2 copy-start.1
  350.6 2.5 copy-start.5
  353.0 1.0 copy-start.18
  361.4 2.1 collective-permute-start.6
  363.6 7.6 collective-permute-start.7
  371.2 8.2 %collective-permute-start.8 = (f32[4,128,4]{0,2,1:T(4,128)S(1)}, f32[4,128,4]{0,2,1:T(4,128)S(1)}, u32[]{:S(2)}, u32[]{:S(2)}) collective-permute-start(f32[4,128,4]{0,2,1:T(4,128)S(1)} %max.47), channel_id=1, source_target_pairs={{0,16},{4,20},{8,24},{12,28},{16,0},{20,4},{24,8},{28,12},{32,48},... | collective-permute-start | bytes 24584 | tf_op jit(solution)/shard_map/ppermute | solution.py:22
  379.5 5.9 collective-permute-start.9
  385.5 13.8 %collective-permute-start.10 = (f32[4,128,4]{0,2,1:T(4,128)S(1)}, f32[4,128,4]{0,2,1:T(4,128)S(1)}, u32[]{:S(2)}, u32[]{:S(2)}) collective-permute-start(f32[4,128,4]{0,2,1:T(4,128)S(1)} %max.49), channel_id=1, source_target_pairs={{0,64},{4,68},{8,72},{12,76},{16,80},{20,84},{24,88},{28,92},{32,9... | collective-permute-start | bytes 24584 | tf_op jit(solution)/shard_map/ppermute | solution.py:22
  399.4 14.7 %collective-permute-start.11 = (f32[4,128,4]{0,2,1:T(4,128)S(1)}, f32[4,128,4]{0,2,1:T(4,128)}, u32[]{:S(2)}, u32[]{:S(2)}) collective-permute-start(f32[4,128,4]{0,2,1:T(4,128)S(1)} %max.50), channel_id=1, source_target_pairs={{0,128},{4,132},{8,136},{12,140},{16,144},{20,148},{24,152},{28,15... | collective-permute-start | bytes 24584 | tf_op jit(solution)/shard_map/ppermute | solution.py:22
  415.2 0.7 copy-start.9
  429.2 255.1 %all-reduce.12.cloned.1.call-start = ((), (), s32[]{:S(2)}) async-start(), calls=%async_computation.4 | async-start | bytes 4194304 | tf_op jit(solution)/shard_map/psum | solution.py:36
  611.8 4.4 slice-start.1
  616.4 2.4 copy-start.11
  620.6 65.9 %copy-start.15 = (f32[1024]{0:T(1024)S(1)}, f32[1024]{0:T(1024)}, u32[]{:S(2)}) copy-start(f32[1024]{0:T(1024)} %param.28) | copy-start | bytes 12292
  620.6 140.6 %all-reduce.14.cloned.1.call-start = ((), (), s32[]{:S(2)}) async-start(), calls=%async_computation.5 | async-start | bytes 4194304 | tf_op jit(solution)/shard_map/psum | solution.py:36
  684.4 2.2 copy-start.2
  697.5 63.8 %copy-start.6 = (bf16[512,1024]{1,0:T(8,128)(2,1)S(1)}, bf16[512,1024]{1,0:T(8,128)(2,1)}, u32[]{:S(2)}) copy-start(bf16[512,1024]{1,0:T(8,128)(2,1)} %multiply_convert_fusion) | copy-start | bytes 3145732
Sparse Core Ops, SparseCore 0:
  9.1 30.0 all-gather.1
  88.8 184.3 all-reduce.5
  286.9 63.5 all-reduce.7
  429.4 182.3 all-reduce.9
  620.8 63.5 all-reduce.11
  697.6 63.5 all-reduce.13
where the time goes:
time: 781 us; the launch traced here: 771 us
  waiting for transfers between devices  605 us (77%)
  local copies, waits for them, and re-layouts  61.7 us (8%)
  matrix products  38.2 us (5%)
  starting transfers between devices  29.7 us (4%)
  other arithmetic  22.4 us (3%)
  between operations  14.1 us (2%)
    psum x2, waiting for transfers between devices, global_totals(): packed = lax.psum(packed, 'seq')  362 us
    psum x3, waiting for transfers between devices, reduce_norm(): total = lax.psum(partial_value, 'tensor')  182 us
    ppermute x12, waiting for transfers between devices, global_max(): result = jnp.maximum(result, lax.ppermute(result, 'seq', pairs))  36.4 us
    ppermute x12, starting transfers between devices, global_max(): result = jnp.maximum(result, lax.ppermute(result, 'seq', pairs))  28.8 us
    all_gather x1, waiting for transfers between devices, on_device(): states = lax.all_gather(new_states, 'tensor', axis=2, tiled=True)  24.1 us
  transfers between devices with their start and end apart: 18, of which 16 were waited for; matrix products, arithmetic and copies ran while one was open for 4% of the time, Pallas kernels for 0%

commit v1 on v0

--- a/solution.py
+++ b/solution.py
@@ -2,6 +2,7 @@
 import jax.numpy as jnp
 from jax import lax
 from jax.sharding import PartitionSpec as P
+from jax.lax import axis_size, ppermute
 
 HEAD_DIM = 64
 EPSILON = 1e-05
@@ -33,7 +34,11 @@
 
 def reduce_norm(residual, partial_value, gain):
     width = residual.shape[1]
-    total = lax.psum(partial_value, "tensor")
+    axis_len = axis_size("tensor")
+    total = partial_value
+    for h in [[(pp, pp ^ k) for pp in range(axis_len)] for k in (1, 2, 4, 8, 16) if k < axis_len]:
+        e_next = ppermute(total, "tensor", h)
+        total = total + e_next
     full = layer_norm(residual.astype(jnp.float32) + total, gain).astype(jnp.bfloat16)
     columns = width // lax.axis_size("tensor")
     return (full, lax.dynamic_slice_in_dim(full, lax.axis_index("tensor") * columns, columns, 1))

time: 781 us -> 864 us (1.11)
  the two profiles are of different devices: /device:TPU:1 before, /device:TPU:128 now
where the time goes in v1:
time: 864 us; the launch traced here: 855 us
  waiting for transfers between devices  712 us (82%)
  local copies, waits for them, and re-layouts  47.2 us (5%)
  matrix products  33.4 us (4%)
  other arithmetic  26.6 us (3%)
  starting transfers between devices  22.2 us (3%)
  between operations  13.8 us (2%)
    psum x2, waiting for transfers between devices, global_totals(): packed = lax.psum(packed, 'seq')  356 us
    ppermute x6, waiting for transfers between devices, reduce_norm(): e_next = ppermute(total, 'tensor', h)  270 us
    ppermute x12, waiting for transfers between devices, global_max(): result = jnp.maximum(result, lax.ppermute(result, 'seq', pairs))  61.7 us
    all_gather x1, waiting for transfers between devices, on_device(): states = lax.all_gather(new_states, 'tensor', axis=2, tiled=True)  23.4 us
  transfers between devices with their start and end apart: 21, of which 21 were waited for; matrix products, arithmetic and copies ran while one was open for 3% of the time, Pallas kernels for 0%

profile of v1, /device:TPU:128, one launch (start us, length us, event | category | flops | bytes accessed | tf_op | source)
XLA Modules:
  0.0 855.1 jit_solution(4368770984354838285)
XLA Ops:
  7.3 3.9 fusion.134
  11.2 2.7 copy.115
  15.2 23.4 %all-gather.2.cloned.1.call-done = bf16[4,128,1024]{2,1,0:T(8,128)(2,1)} async-done(((bf16[4,128,256]{2,1,0:T(8,128)(2,1)}), bf16[4,128,1024]{2,1,0:T(8,128)(2,1)}) %all-gather.2.cloned.1.call-update) | async-done | bytes 1048592 | tf_op jit(solution)/shard_map/all_gather | solution.py:67
  41.6 2.0 select_reduce_fusion.2
  43.8 2.2 convolution_convert_fusion.3
  46.0 2.0 reshape.291
  48.0 3.0 fusion.59
  55.6 2.2 collective-permute-done.1
  57.8 3.0 collective-permute-start.2
  60.8 2.1 collective-permute-done.2
  63.6 3.0 collective-permute-done.3
  67.3 2.6 copy.164
  72.0 2.2 convolution_convert_fusion.2
  74.2 2.0 reshape.292
  76.2 2.6 collective-permute-done.5
  79.5 2.4 convolution_bitcast_fusion.3
  86.8 1.9 pad_maximum_fusion
  90.7 1.9 fusion.57
  93.9 175.8 %all-reduce.3.cloned.1.call-done = f32[133120]{0:T(1024)} async-done(((f32[133120]{0:T(1024)}), f32[133120]{0:T(1024)}) %all-reduce.3.cloned.1.call-update) | async-done | bytes 532496 | tf_op jit(solution)/shard_map/psum | solution.py:30
  271.7 1.9 slice.54
  279.9 46.9 %collective-permute-done.6 = f32[512,1024]{1,0:T(8,128)S(1)} collective-permute-done((f32[512,1024]{1,0:T(8,128)S(1)}, f32[512,1024]{1,0:T(8,128)S(1)}, u32[]{:S(2)}, u32[]{:S(2)}) %collective-permute-start.6) | collective-permute-done | bytes 2097184 | tf_op jit(solution)/shard_map/ppermute | solution.py:40
  326.8 1.7 add.127
  328.6 3.0 collective-permute-start.7
  331.5 2.1 fusion.135
  335.1 2.5 copy.145
  337.8 40.2 %collective-permute-done.7 = f32[512,1024]{1,0:T(8,128)} collective-permute-done((f32[512,1024]{1,0:T(8,128)}, f32[512,1024]{1,0:T(8,128)}, u32[]{:S(2)}, u32[]{:S(2)}) %collective-permute-start.7) | collective-permute-done | bytes 2097184 | tf_op jit(solution)/shard_map/ppermute | solution.py:40
  378.0 3.0 fusion.133
  383.9 3.1 select_reduce_fusion
  388.8 8.3 collective-permute-done.9
  397.7 8.6 %collective-permute-done.10 = f32[4,128,4]{0,2,1:T(4,128)S(1)} collective-permute-done((f32[4,128,4]{0,2,1:T(4,128)S(1)}, f32[4,128,4]{0,2,1:T(4,128)S(1)}, u32[]{:S(2)}, u32[]{:S(2)}) %collective-permute-start.10) | collective-permute-done | bytes 8224 | tf_op jit(solution)/shard_map/ppermute | solution.py:23
  406.6 6.6 collective-permute-done.11
  413.4 12.3 %collective-permute-done.12 = f32[4,128,4]{0,2,1:T(4,128)S(1)} collective-permute-done((f32[4,128,4]{0,2,1:T(4,128)S(1)}, f32[4,128,4]{0,2,1:T(4,128)S(1)}, u32[]{:S(2)}, u32[]{:S(2)}) %collective-permute-start.12) | collective-permute-done | bytes 8224 | tf_op jit(solution)/shard_map/ppermute | solution.py:23
  426.3 2.5 copy.147
  428.8 11.9 %collective-permute-done.13 = f32[4,128,4]{0,2,1:T(4,128)} collective-permute-done((f32[4,128,4]{0,2,1:T(4,128)S(1)}, f32[4,128,4]{0,2,1:T(4,128)}, u32[]{:S(2)}, u32[]{:S(2)}) %collective-permute-start.13) | collective-permute-done | bytes 8224 | tf_op jit(solution)/shard_map/ppermute | solution.py:23
  441.8 2.4 fusion.48
  448.1 1.9 pad_maximum_fusion.1
  450.0 180.2 %all-reduce.5.cloned.1.call-done = f32[133120]{0:T(1024)} async-done(((f32[133120]{0:T(1024)}), f32[133120]{0:T(1024)}) %all-reduce.5.cloned.1.call-update) | async-done | bytes 532496 | tf_op jit(solution)/shard_map/psum | solution.py:30
  630.1 1.9 slice.56
  637.2 46.9 %collective-permute-done.14 = f32[512,1024]{1,0:T(8,128)S(1)} collective-permute-done((f32[512,1024]{1,0:T(8,128)S(1)}, f32[512,1024]{1,0:T(8,128)S(1)}, u32[]{:S(2)}, u32[]{:S(2)}) %collective-permute-start.14) | collective-permute-done | bytes 2097184 | tf_op jit(solution)/shard_map/ppermute | solution.py:40
  684.5 3.3 collective-permute-start.15
  687.8 46.2 %collective-permute-done.15 = f32[512,1024]{1,0:T(8,128)S(1)} collective-permute-done((f32[512,1024]{1,0:T(8,128)S(1)}, f32[512,1024]{1,0:T(8,128)S(1)}, u32[]{:S(2)}, u32[]{:S(2)}) %collective-permute-start.15) | collective-permute-done | bytes 2097184 | tf_op jit(solution)/shard_map/ppermute | solution.py:40
  734.0 1.9 fusion.132
  735.9 9.8 %fusion.16 = f32[512,1024]{1,0:T(8,128)} fusion(bf16[1024,1024]{1,0:T(8,128)(2,1)S(1)} %copy-done, bf16[1024,1024]{1,0:T(8,128)(2,1)} %param.25, f32[512,1024]{1,0:T(8,128)} %get-tuple-element.14, f32[1024]{0:T(1024)S(1)} %copy-done.11, f32[512]{0:T(512)S(1)} %get-tuple-element.25, f32[512]{0:T(512)S(1)} %get-tuple-element.24), kind=kOutput, calls=%fused_computation.49 | convolution fusion | flops 2183659520 | bytes 8396800 | tf_op jit(solution)/shard_map/dot_general | solution.py:197
  747.2 45.5 %collective-permute-done.16 = f32[512,1024]{1,0:T(8,128)S(1)} collective-permute-done((f32[512,1024]{1,0:T(8,128)}, f32[512,1024]{1,0:T(8,128)S(1)}, u32[]{:S(2)}, u32[]{:S(2)}) %collective-permute-start.16) | collective-permute-done | bytes 2097184 | tf_op jit(solution)/shard_map/ppermute | solution.py:40
  792.7 3.3 add.137
  796.0 3.0 collective-permute-start.17
  799.7 44.0 %collective-permute-done.17 = f32[512,1024]{1,0:T(8,128)} collective-permute-done((f32[512,1024]{1,0:T(8,128)}, f32[512,1024]{1,0:T(8,128)}, u32[]{:S(2)}, u32[]{:S(2)}) %collective-permute-start.17) | collective-permute-done | bytes 2097184 | tf_op jit(solution)/shard_map/ppermute | solution.py:40
  843.8 3.6 fusion.131
  (136 shorter events, 51.7 us)
Async XLA Ops:
  6.5 729.3 %copy-start = (bf16[1024,1024]{1,0:T(8,128)(2,1)S(1)}, bf16[1024,1024]{1,0:T(8,128)(2,1)}, u32[]{:S(2)}) copy-start(bf16[1024,1024]{1,0:T(8,128)(2,1)} %param.26) | copy-start | bytes 6291460
  6.5 32.1 %all-gather.2.cloned.1.call-start = ((), (), s32[]{:S(2)}) async-start(), calls=%async_computation | async-start | bytes 1310720 | tf_op jit(solution)/shard_map/all_gather | solution.py:67
  7.3 262.4 %all-reduce.3.cloned.1.call-start = ((), (), s32[]{:S(2)}) async-start(), calls=%async_computation.1 | async-start | bytes 1064960 | tf_op jit(solution)/shard_map/psum | solution.py:30
  11.2 2.7 copy-start.8
  11.2 3.3 copy-start.15
  11.2 3.9 copy-start.9
  11.2 27.4 %copy-start.13 = (bf16[1024,256]{1,0:T(8,128)(2,1)S(1)}, bf16[1024,256]{1,0:T(8,128)(2,1)}, u32[]{:S(2)}) copy-start(bf16[1024,256]{1,0:T(8,128)(2,1)} %param.19) | copy-start | bytes 1572868
  40.3 3.5 copy-start.3
  52.8 1.3 collective-permute-start
  54.1 3.7 collective-permute-start.1
  57.8 5.2 collective-permute-start.2
  62.9 3.7 collective-permute-start.3
  66.6 4.7 collective-permute-start.4
  71.3 7.6 collective-permute-start.5
  88.7 541.5 %all-reduce.5.cloned.1.call-start = ((), (), s32[]{:S(2)}) async-start(), calls=%async_computation.2 | async-start | bytes 1064960 | tf_op jit(solution)/shard_map/psum | solution.py:30
  276.3 1.6 copy-start.6
  278.3 48.5 %collective-permute-start.6 = (f32[512,1024]{1,0:T(8,128)S(1)}, f32[512,1024]{1,0:T(8,128)S(1)}, u32[]{:S(2)}, u32[]{:S(2)}) collective-permute-start(f32[512,1024]{1,0:T(8,128)S(1)} %fusion.69), channel_id=1, source_target_pairs={{0,1},{1,0},{2,3},{3,2},{4,5},{5,4},{6,7},{7,6},{8,9},{9,8},{10,11... | collective-permute-start | bytes 6291464 | tf_op jit(solution)/shard_map/ppermute | solution.py:40
  328.6 49.5 %collective-permute-start.7 = (f32[512,1024]{1,0:T(8,128)}, f32[512,1024]{1,0:T(8,128)}, u32[]{:S(2)}, u32[]{:S(2)}) collective-permute-start(f32[512,1024]{1,0:T(8,128)} %add.127), channel_id=1, source_target_pairs={{0,2},{1,3},{2,0},{3,1},{4,6},{5,7},{6,4},{7,5},{8,10},{9,11},{10,... | collective-permute-start | bytes 6291464 | tf_op jit(solution)/shard_map/ppermute | solution.py:40
  331.5 6.1 copy-start.12
  337.7 44.6 %copy-start.10 = (f32[1024]{0:T(1024)S(1)}, f32[1024]{0:T(1024)}, u32[]{:S(2)}) copy-start(f32[1024]{0:T(1024)} %param.27) | copy-start | bytes 12292
  337.8 44.6 %copy-start.14 = (bf16[1024,256]{1,0:T(8,128)(2,1)S(1)}, bf16[1024,256]{1,0:T(8,128)(2,1)}, u32[]{:S(2)}) copy-start(bf16[1024,256]{1,0:T(8,128)(2,1)} %param.23) | copy-start | bytes 1572868
  381.0 1.3 copy-start.1
  387.0 1.6 collective-permute-start.8
  388.7 8.4 collective-permute-start.9
  397.2 9.1 %collective-permute-start.10 = (f32[4,128,4]{0,2,1:T(4,128)S(1)}, f32[4,128,4]{0,2,1:T(4,128)S(1)}, u32[]{:S(2)}, u32[]{:S(2)}) collective-permute-start(f32[4,128,4]{0,2,1:T(4,128)S(1)} %max.47), channel_id=1, source_target_pairs={{0,16},{4,20},{8,24},{12,28},{16,0},{20,4},{24,8},{28,12},{32,48},... | collective-permute-start | bytes 24584 | tf_op jit(solution)/shard_map/ppermute | solution.py:23
  406.3 6.9 collective-permute-start.11
  413.3 12.4 %collective-permute-start.12 = (f32[4,128,4]{0,2,1:T(4,128)S(1)}, f32[4,128,4]{0,2,1:T(4,128)S(1)}, u32[]{:S(2)}, u32[]{:S(2)}) collective-permute-start(f32[4,128,4]{0,2,1:T(4,128)S(1)} %max.49), channel_id=1, source_target_pairs={{0,64},{4,68},{8,72},{12,76},{16,80},{20,84},{24,88},{28,92},{32,9... | collective-permute-start | bytes 24584 | tf_op jit(solution)/shard_map/ppermute | solution.py:23
  425.8 15.0 %collective-permute-start.13 = (f32[4,128,4]{0,2,1:T(4,128)S(1)}, f32[4,128,4]{0,2,1:T(4,128)}, u32[]{:S(2)}, u32[]{:S(2)}) collective-permute-start(f32[4,128,4]{0,2,1:T(4,128)S(1)} %max.50), channel_id=1, source_target_pairs={{0,128},{4,132},{8,136},{12,140},{16,144},{20,148},{24,152},{28,15... | collective-permute-start | bytes 24584 | tf_op jit(solution)/shard_map/ppermute | solution.py:23
  428.8 15.4 %copy-start.4 = (f32[4,128,4,8]{3,0,2,1:T(4,128)S(1)}, f32[4,128,4,8]{3,0,2,1:T(4,128)}, u32[]{:S(2)}) copy-start(f32[4,128,4,8]{3,0,2,1:T(4,128)} %get-tuple-element.33) | copy-start | bytes 196612
  428.8 15.4 %copy-start.5 = (bf16[128,8,4,64]{3,1,2,0:T(8,128)(2,1)S(1)}, bf16[128,8,4,64]{3,1,2,0:T(8,128)(2,1)}, u32[]{:S(2)}) copy-start(bf16[128,8,4,64]{3,1,2,0:T(8,128)(2,1)} %copy.147) | copy-start | bytes 1572868
  630.1 3.4 slice-start
  633.8 1.3 copy-start.7
  635.6 98.4 %copy-start.2 = (f32[512,1024]{1,0:T(8,128)S(1)}, f32[512,1024]{1,0:T(8,128)}, u32[]{:S(2)}) copy-start(f32[512,1024]{1,0:T(8,128)} %copy-done.1) | copy-start | bytes 6291460
  635.6 48.5 %collective-permute-start.14 = (f32[512,1024]{1,0:T(8,128)S(1)}, f32[512,1024]{1,0:T(8,128)S(1)}, u32[]{:S(2)}, u32[]{:S(2)}) collective-permute-start(f32[512,1024]{1,0:T(8,128)S(1)} %fusion.66), channel_id=1, source_target_pairs={{0,1},{1,0},{2,3},{3,2},{4,5},{5,4},{6,7},{7,6},{8,9},{9,8},{10,11... | collective-permute-start | bytes 6291464 | tf_op jit(solution)/shard_map/ppermute | solution.py:40
  684.5 51.4 %copy-start.11 = (f32[1024]{0:T(1024)S(1)}, f32[1024]{0:T(1024)}, u32[]{:S(2)}) copy-start(f32[1024]{0:T(1024)} %param.28) | copy-start | bytes 12292
  684.5 49.5 %collective-permute-start.15 = (f32[512,1024]{1,0:T(8,128)S(1)}, f32[512,1024]{1,0:T(8,128)S(1)}, u32[]{:S(2)}, u32[]{:S(2)}) collective-permute-start(f32[512,1024]{1,0:T(8,128)S(1)} %add.133), channel_id=1, source_target_pairs={{0,2},{1,3},{2,0},{3,1},{4,6},{5,7},{6,4},{7,5},{8,10},{9,11},{10,... | collective-permute-start | bytes 6291464 | tf_op jit(solution)/shard_map/ppermute | solution.py:40
  745.7 47.0 %collective-permute-start.16 = (f32[512,1024]{1,0:T(8,128)}, f32[512,1024]{1,0:T(8,128)S(1)}, u32[]{:S(2)}, u32[]{:S(2)}) collective-permute-start(f32[512,1024]{1,0:T(8,128)} %fusion.16), channel_id=1, source_target_pairs={{0,1},{1,0},{2,3},{3,2},{4,5},{5,4},{6,7},{7,6},{8,9},{9,8},{10,11... | collective-permute-start | bytes 6291464 | tf_op jit(solution)/shard_map/ppermute | solution.py:40
  796.0 47.8 %collective-permute-start.17 = (f32[512,1024]{1,0:T(8,128)}, f32[512,1024]{1,0:T(8,128)}, u32[]{:S(2)}, u32[]{:S(2)}) collective-permute-start(f32[512,1024]{1,0:T(8,128)} %add.137), channel_id=1, source_target_pairs={{0,2},{1,3},{2,0},{3,1},{4,6},{5,7},{6,4},{7,5},{8,10},{9,11},{10,... | collective-permute-start | bytes 6291464 | tf_op jit(solution)/shard_map/ppermute | solution.py:40
Sparse Core Ops, SparseCore 0:
  9.1 29.4 all-gather.1
  88.8 180.8 all-reduce.2
  450.1 179.9 all-reduce.4
